TPU v7x, 512 devices: a whole 4x4x16 slice. The times are simulated.
512 devices in a mesh: seq: 128 (over x, z, y_hi), batch: 4 (over y_lo, core).
Axes of the slice: x: 4, y: 4 (y_hi: 2, y_lo: 2; y = y_hi * 2 + y_lo), z: 16, core: 2. Of those that a mesh axis runs over, the one named last changes fastest.
Arguments:
- inputs: bfloat16 [4, 128, 16384], P('batch', None, 'seq'), may hold values from -6 to 6
- out_grad: bfloat16 [4, 128, 16384], P('batch', None, 'seq'), may hold values from -0.046875 to 0.046875
- filters: float32 [128, 16384], P(None, 'seq'), may hold values from -6 to 6
Outputs:
- in_grad: bfloat16 [4, 128, 16384], P('batch', None, 'seq')
- filter_grad: float32 [128, 16384], P(None, 'seq')
All inputs are finite; a program needn't handle non-finite values.
Results may differ from a plain program's by a relative error of at most 0.0025.
Values sent between devices are 32-bit elements; how exact they have to be, the bound alone decides.
No kernel may reach another device: no remote copies, remote signals or barrier semaphores. Data moves between devices by JAX's collectives and lax.ppermute only.
A program may use at most 64 MiB of HBM per device.

v0:
```python
import math
import jax
import jax.numpy as jnp
from jax import lax
from jax.sharding import PartitionSpec as P

FACTOR = 16


def contract(pattern, operand, weights):
    return jnp.einsum(
        pattern,
        operand,
        weights,
        precision=lax.Precision.HIGHEST,
        preferred_element_type=jnp.float32,
    )


def angles(left_index, right_index, modulus):
    product = left_index[:, None] * right_index[None, :] % modulus
    return product.astype(jnp.float32) * (2.0 * math.pi / modulus)


def rotate(pattern, real_part, imag_part, angle_table, orient):
    cosine = jnp.cos(angle_table)
    sine_part = jnp.sin(angle_table)
    new_real = contract(pattern, real_part, cosine) - orient * contract(
        pattern, imag_part, sine_part
    )
    new_imag = contract(pattern, imag_part, cosine) + orient * contract(
        pattern, real_part, sine_part
    )
    return (new_real, new_imag)


def twist(real_part, imag_part, angle_table, orient):
    cosine = jnp.cos(angle_table)
    sine_part = jnp.sin(angle_table)
    return (
        real_part * cosine - orient * imag_part * sine_part,
        imag_part * cosine + orient * real_part * sine_part,
    )


def local_tables(length_all):
    inner = length_all // FACTOR
    outer_index = jnp.arange(FACTOR, dtype=jnp.int32)
    inner_index = jnp.arange(inner, dtype=jnp.int32)
    outer_table = angles(outer_index, outer_index, FACTOR)
    mid_table = angles(outer_index, inner_index, length_all)
    inner_table = angles(inner_index, inner_index, inner)
    return (outer_table, mid_table, inner_table)


def local_forward(real_part, imag_part):
    row_count, held, length_all = real_part.shape
    outer_table, mid_table, inner_table = local_tables(length_all)
    real_part = real_part.reshape(row_count, held, FACTOR, length_all // FACTOR)
    imag_part = imag_part.reshape(row_count, held, FACTOR, length_all // FACTOR)
    real_part, imag_part = rotate("kiuv,uq->kiqv", real_part, imag_part, outer_table, -1.0)
    real_part, imag_part = twist(real_part, imag_part, mid_table, -1.0)
    return rotate("kiqv,vm->kiqm", real_part, imag_part, inner_table, -1.0)


def local_inverse(real_part, imag_part):
    row_count, held, outer, inner = real_part.shape
    outer_table, mid_table, inner_table = local_tables(outer * inner)
    real_part, imag_part = rotate("kiqm,mv->kiqv", real_part, imag_part, inner_table, 1.0)
    real_part, imag_part = twist(real_part, imag_part, mid_table, 1.0)
    real_part, imag_part = rotate("kiqv,qu->kiuv", real_part, imag_part, outer_table, 1.0)
    return (
        real_part.reshape(row_count, held, outer * inner),
        imag_part.reshape(row_count, held, outer * inner),
    )


def body(inputs, out_grad, filters):
    seq_count = lax.axis_size("seq")
    position = lax.axis_index("seq")
    length_dev = inputs.shape[2]
    block_len = length_dev // seq_count
    total_len = 2 * seq_count * length_dev
    channels = inputs.shape[1]
    stacked = jnp.concatenate(
        [inputs[0].astype(jnp.float32), out_grad[0].astype(jnp.float32), filters], axis=0
    )
    row_count = stacked.shape[0]
    spread = lax.all_to_all(
        stacked.reshape(row_count, seq_count, block_len),
        "seq",
        split_axis=1,
        concat_axis=1,
        tiled=True,
    )
    low_index = jnp.arange(seq_count, dtype=jnp.int32)
    second_freq = jnp.where(low_index == 0, seq_count, 2 * seq_count - low_index)
    freq_order = jnp.stack([low_index, second_freq], axis=1).reshape(2 * seq_count)
    cross_table = angles(low_index, freq_order, 2 * seq_count)
    local_cols = position * block_len + jnp.arange(block_len, dtype=jnp.int32)
    cols_twist = angles(freq_order, local_cols, total_len)
    real_part = contract("kaj,am->kmj", spread, jnp.cos(cross_table))
    imag_part = -contract("kaj,am->kmj", spread, jnp.sin(cross_table))
    real_part, imag_part = twist(real_part, imag_part, cols_twist, -1.0)
    cols_real, cols_imag = (
        lax.all_to_all(real_part, "seq", split_axis=1, concat_axis=2, tiled=True),
        lax.all_to_all(imag_part, "seq", split_axis=1, concat_axis=2, tiled=True),
    )
    spec_real, spec_imag = local_forward(cols_real, cols_imag)
    input_real = spec_real[:channels]
    input_imag = spec_imag[:channels]
    grad_real = spec_real[channels : 2 * channels]
    grad_imag = spec_imag[channels : 2 * channels]
    filter_real = spec_real[2 * channels :]
    filter_imag = spec_imag[2 * channels :]
    first_real = filter_real * grad_real + filter_imag * grad_imag
    first_imag = filter_real * grad_imag - filter_imag * grad_real
    second_real = input_real * grad_real + input_imag * grad_imag
    second_imag = input_real * grad_imag - input_imag * grad_real
    joined_real = jnp.concatenate([first_real, second_real], axis=0)
    joined_imag = jnp.concatenate([first_imag, second_imag], axis=0)
    held_freq = lax.dynamic_slice_in_dim(freq_order, 2 * position, 2)
    all_cols = jnp.arange(length_dev, dtype=jnp.int32)
    back_twist = angles(held_freq, all_cols, total_len)
    back_table = angles(freq_order, low_index, 2 * seq_count)
    factor_scale = 1.0 / total_len
    cos_back = jnp.cos(back_table) * factor_scale
    sin_back = jnp.sin(back_table) * factor_scale
    back_real, back_imag = local_inverse(joined_real, joined_imag)
    back_real, back_imag = twist(back_real, back_imag, back_twist, 1.0)
    gath_real, gath_imag = (
        lax.all_to_all(back_real, "seq", split_axis=2, concat_axis=1, tiled=True),
        lax.all_to_all(back_imag, "seq", split_axis=2, concat_axis=1, tiled=True),
    )
    rebuilt = contract("kmj,ma->kaj", gath_real, cos_back) - contract(
        "kmj,ma->kaj", gath_imag, sin_back
    )
    returned = lax.all_to_all(rebuilt, "seq", split_axis=1, concat_axis=2, tiled=True)[:, 0, :]
    in_grad = returned[:channels].astype(jnp.bfloat16)[None]
    partial_grad = returned[channels:]
    filter_grad = lax.psum(partial_grad, "batch")
    return (in_grad, filter_grad)


def solution(mesh):
    placed = (P("batch", None, "seq"), P("batch", None, "seq"), P(None, "seq"))
    return jax.shard_map(
        body,
        mesh=mesh,
        in_specs=placed,
        out_specs=(P("batch", None, "seq"), P(None, "seq")),
        check_vma=False,
    )
```

profile of v0, /device:TPU:1, one launch (start us, length us, event | category | flops | bytes accessed | tf_op | source)
XLA Modules:
  0.0 269.2 jit_solution(8236200142034256242)
XLA Ops:
  7.2 0.0 copy-start.1
  7.2 0.0 copy-start
  7.2 0.9 copy.67
  8.1 0.0 copy-done.1
  8.1 0.1 copy.68
  8.2 0.0 copy-done
  8.2 0.1 copy.69
  8.4 0.8 reshape.208
  9.2 23.0 %all-to-all-start = ((f32[384,128,1]{0,2,1:T(1,128)}), f32[384,128,1]{0,2,1:T(1,128)S(1)}, u32[]{:S(2)}, u32[]{:S(2)}) async-start(f32[384,128,1]{0,2,1:T(1,128)} %reshape.208), calls=%async_computation | async-start | bytes 393216 | tf_op jit(solution)/shard_map/all_to_all | solution.py:89
  32.2 0.1 copy.66
  32.3 0.1 mul.547
  32.4 0.1 fusion.201
  32.5 19.3 %all-to-all-done = f32[384,128,1]{0,2,1:T(1,128)S(1)} async-done(((f32[384,128,1]{0,2,1:T(1,128)}), f32[384,128,1]{0,2,1:T(1,128)S(1)}, u32[]{:S(2)}, u32[]{:S(2)}) %all-to-all-start) | async-done | bytes 196640 | tf_op jit(solution)/shard_map/all_to_all | solution.py:89
  51.8 1.0 fusion
  52.8 1.0 add_bitcast_fusion.1
  53.8 1.2 copy.70
  55.0 7.5 %all-to-all-start.1 = ((f32[384,256,1]{0,2,1:T(1,128)}), f32[384,256,1]{0,2,1:T(1,128)S(1)}, u32[]{:S(2)}, u32[]{:S(2)}) async-start(f32[384,256,1]{0,2,1:T(1,128)} %copy.70), calls=%async_computation.1 | async-start | bytes 786432 | tf_op jit(solution)/shard_map/all_to_all | solution.py:106
  62.5 1.1 copy.73
  63.6 23.8 %all-to-all-done.1 = f32[384,256,1]{0,2,1:T(1,128)S(1)} async-done(((f32[384,256,1]{0,2,1:T(1,128)}), f32[384,256,1]{0,2,1:T(1,128)S(1)}, u32[]{:S(2)}, u32[]{:S(2)}) %all-to-all-start.1) | async-done | bytes 393248 | tf_op jit(solution)/shard_map/all_to_all | solution.py:106
  87.4 10.3 %all-to-all-start.2 = ((f32[384,256,1]{0,2,1:T(1,128)}), f32[384,256,1]{0,2,1:T(1,128)S(1)}, u32[]{:S(2)}, u32[]{:S(2)}) async-start(f32[384,256,1]{0,2,1:T(1,128)} %copy.73), calls=%async_computation.2 | async-start | bytes 786432 | tf_op jit(solution)/shard_map/all_to_all | solution.py:107
  97.7 0.1 broadcast_multiply_fusion
  97.7 0.1 copy.82
  97.8 0.1 fusion.105
  97.9 0.1 copy.83
  97.9 0.1 dynamic_slice.3
  98.0 0.1 fusion.114
  98.2 0.5 convolution_multiply_fusion.2
  98.7 23.6 %all-to-all-done.2 = f32[384,256,1]{0,2,1:T(1,128)S(1)} async-done(((f32[384,256,1]{0,2,1:T(1,128)}), f32[384,256,1]{0,2,1:T(1,128)S(1)}, u32[]{:S(2)}, u32[]{:S(2)}) %all-to-all-start.2) | async-done | bytes 393248 | tf_op jit(solution)/shard_map/all_to_all | solution.py:107
  122.3 0.5 convolution_multiply_fusion.3
  122.9 0.5 convolution_add_fusion.1
  123.4 0.6 add_bitcast_fusion
  124.0 0.6 convolution_multiply_fusion.1
  124.6 0.6 convolution_multiply_fusion
  125.2 0.6 convolution_subtract_fusion
  125.8 0.6 convolution_add_fusion
  126.3 0.1 multiply_subtract_fusion.2
  126.4 0.4 fusion.20
  126.8 0.4 fusion.21
  127.2 0.4 convolution_subtract_fusion.3
  127.6 0.5 multiply_subtract_fusion
  128.1 0.4 fusion.18
  128.5 0.4 fusion.14
  129.0 0.4 fusion.2
  129.4 0.4 fusion.1
  129.8 0.3 fusion.13
  130.1 0.9 copy.90
  131.0 10.1 %all-to-all-start.3 = ((f32[256,2,128]{0,1,2:T(2,128)}), f32[256,2,128]{0,1,2:T(2,128)S(1)}, u32[]{:S(2)}, u32[]{:S(2)}) async-start(f32[256,2,128]{0,1,2:T(2,128)} %copy.90), calls=%async_computation.3 | async-start | bytes 524288 | tf_op jit(solution)/shard_map/all_to_all | solution.py:132
  141.2 0.9 copy.91
  142.1 19.4 %all-to-all-done.3 = f32[256,2,128]{0,1,2:T(2,128)S(1)} async-done(((f32[256,2,128]{0,1,2:T(2,128)}), f32[256,2,128]{0,1,2:T(2,128)S(1)}, u32[]{:S(2)}, u32[]{:S(2)}) %all-to-all-start.3) | async-done | bytes 262176 | tf_op jit(solution)/shard_map/all_to_all | solution.py:132
  161.4 9.2 %all-to-all-start.4 = ((f32[256,2,128]{0,1,2:T(2,128)}), f32[256,2,128]{0,1,2:T(2,128)S(1)}, u32[]{:S(2)}, u32[]{:S(2)}) async-start(f32[256,2,128]{0,1,2:T(2,128)} %copy.91), calls=%async_computation.4 | async-start | bytes 524288 | tf_op jit(solution)/shard_map/all_to_all | solution.py:133
  170.7 0.3 all-reduce.2.cloned.1.call-start
  170.9 0.2 reshape.214
  171.1 0.9 fusion.38
  172.1 19.0 %all-to-all-done.4 = f32[256,2,128]{0,1,2:T(2,128)S(1)} async-done(((f32[256,2,128]{0,1,2:T(2,128)}), f32[256,2,128]{0,1,2:T(2,128)S(1)}, u32[]{:S(2)}, u32[]{:S(2)}) %all-to-all-start.4) | async-done | bytes 262176 | tf_op jit(solution)/shard_map/all_to_all | solution.py:133
  191.1 0.2 reshape.215
  191.2 0.9 fusion.3
  192.2 0.1 copy.92
  192.3 25.7 %all_to_all.74 = f32[256,128,1]{0,2,1:T(1,128)S(1)} all-to-all(f32[256,128,1]{0,2,1:T(1,128)S(1)} %copy.92), channel_id=1, replica_groups=mesh['seq'=128,'batch'=4] {'seq'}, dimensions={1} | all-to-all | bytes 262144 | tf_op jit(solution)/shard_map/all_to_all | solution.py:138
  218.0 0.7 slice.46
  218.7 0.0 all-reduce.2.cloned.1.call-update
  218.8 0.7 copy.100
  219.5 41.3 %all-reduce.2.cloned.1.call-done = f32[128,128]{0,1:T(8,128)} async-done(((f32[128,128]{0,1:T(8,128)}), f32[128,128]{0,1:T(8,128)}) %all-reduce.2.cloned.1.call-update) | async-done | bytes 65552 | tf_op jit(solution)/shard_map/psum | solution.py:141
  260.8 1.6 copy.94
  (9 shorter events, 0.2 us)
Async XLA Ops:
  7.2 0.9 copy-start.1
  7.2 1.0 copy-start
  9.2 42.6 %all-to-all-start = ((f32[384,128,1]{0,2,1:T(1,128)}), f32[384,128,1]{0,2,1:T(1,128)S(1)}, u32[]{:S(2)}, u32[]{:S(2)}) async-start(f32[384,128,1]{0,2,1:T(1,128)} %reshape.208), calls=%async_computation | async-start | bytes 393216 | tf_op jit(solution)/shard_map/all_to_all | solution.py:89
  55.0 32.4 %all-to-all-start.1 = ((f32[384,256,1]{0,2,1:T(1,128)}), f32[384,256,1]{0,2,1:T(1,128)S(1)}, u32[]{:S(2)}, u32[]{:S(2)}) async-start(f32[384,256,1]{0,2,1:T(1,128)} %copy.70), calls=%async_computation.1 | async-start | bytes 786432 | tf_op jit(solution)/shard_map/all_to_all | solution.py:106
  87.4 34.9 %all-to-all-start.2 = ((f32[384,256,1]{0,2,1:T(1,128)}), f32[384,256,1]{0,2,1:T(1,128)S(1)}, u32[]{:S(2)}, u32[]{:S(2)}) async-start(f32[384,256,1]{0,2,1:T(1,128)} %copy.73), calls=%async_computation.2 | async-start | bytes 786432 | tf_op jit(solution)/shard_map/all_to_all | solution.py:107
  131.0 30.4 %all-to-all-start.3 = ((f32[256,2,128]{0,1,2:T(2,128)}), f32[256,2,128]{0,1,2:T(2,128)S(1)}, u32[]{:S(2)}, u32[]{:S(2)}) async-start(f32[256,2,128]{0,1,2:T(2,128)} %copy.90), calls=%async_computation.3 | async-start | bytes 524288 | tf_op jit(solution)/shard_map/all_to_all | solution.py:132
  161.4 29.6 %all-to-all-start.4 = ((f32[256,2,128]{0,1,2:T(2,128)}), f32[256,2,128]{0,1,2:T(2,128)S(1)}, u32[]{:S(2)}, u32[]{:S(2)}) async-start(f32[256,2,128]{0,1,2:T(2,128)} %copy.91), calls=%async_computation.4 | async-start | bytes 524288 | tf_op jit(solution)/shard_map/all_to_all | solution.py:133
  170.7 90.1 %all-reduce.2.cloned.1.call-start = ((), (), s32[]{:S(2)}) async-start(), calls=%async_computation.6 | async-start | bytes 131072 | tf_op jit(solution)/shard_map/psum | solution.py:141
Sparse Core Ops, SparseCore 0:
  218.9 41.8 all-reduce.1
where the time goes:
time: 270 us; the launch traced here: 269 us
  waiting for transfers between devices  146 us (54%)
  starting transfers between devices  60.3 us (22%)
  blocking collectives  25.7 us (10%)
  between operations  14.4 us (5%)
  matrix products  11.7 us (4%)
  local copies, waits for them, and re-layouts  10 us (4%)
    psum x1, waiting for transfers between devices, body(): filter_grad = lax.psum(partial_grad, 'batch')  41.3 us
    all_to_all x1, blocking collectives, body(): lax.all_to_all(rebuilt, 'seq', split_axis=1, concat_axis=2, tiled=True)  25.7 us
    all_to_all x1, waiting for transfers between devices, body(): lax.all_to_all(real_part, 'seq', split_axis=1, concat_axis=2, tiled=True)  23.8 us
    all_to_all x1, waiting for transfers between devices, body(): lax.all_to_all(imag_part, 'seq', split_axis=1, concat_axis=2, tiled=True)  23.6 us
    all_to_all x1, starting transfers between devices, body(): lax.all_to_all(stacked.reshape(row_count, seq_count, block_len), 'seq', s...  23 us
    all_to_all x1, waiting for transfers between devices, body(): lax.all_to_all(back_real, 'seq', split_axis=2, concat_axis=1, tiled=True)  19.4 us
    all_to_all x1, waiting for transfers between devices, body(): lax.all_to_all(stacked.reshape(row_count, seq_count, block_len), 'seq', s...  19.3 us
    all_to_all x1, waiting for transfers between devices, body(): lax.all_to_all(back_imag, 'seq', split_axis=2, concat_axis=1, tiled=True)  19 us
  transfers between devices with their start and end apart: 6, of which 6 were waited for; matrix products, arithmetic and copies ran while one was open for 2% of the time, Pallas kernels for 0%

commit v1 on v0

--- a/solution.py
+++ b/solution.py
@@ -138,7 +138,7 @@
     returned = lax.all_to_all(rebuilt, "seq", split_axis=1, concat_axis=2, tiled=True)[:, 0, :]
     in_grad = returned[:channels].astype(jnp.bfloat16)[None]
     partial_grad = returned[channels:]
-    filter_grad = lax.psum(partial_grad, "batch")
+    filter_grad = jnp.sum(lax.all_gather(partial_grad, "batch"), axis=0)
     return (in_grad, filter_grad)
 
 

time: 270 us -> 223 us (0.83)
  waiting for transfers between devices: 146 us -> 105 us
  between operations: 14.4 us -> 1 us
  blocking collectives: 25.7 us -> 35 us
    psum x1 -> x0, waiting for transfers between devices: 41.3 us -> none  [body(): filter_grad = lax.psum(partial_grad, 'batch')]
    all_gather x0 -> x1, blocking collectives: none -> 9.28 us  [body(): filter_grad = jnp.sum(lax.all_gather(partial_grad, 'batch'), axis=0)]
  transfers between devices with their start and end apart: 6 -> 5, of which waited for: 6 -> 5; matrix products, arithmetic and copies ran while one was open for 2% -> 2% of each run, Pallas kernels for 0% -> 0%
where the time goes in v1:
time: 223 us
  waiting for transfers between devices  105 us (47%)
  starting transfers between devices  59.9 us (27%)
  blocking collectives  35 us (16%)
  matrix products  11.7 us (5%)
  local copies, waits for them, and re-layouts  8.62 us (4%)
    all_to_all x1, blocking collectives, body(): lax.all_to_all(rebuilt, 'seq', split_axis=1, concat_axis=2, tiled=True)  25.7 us
    all_to_all x1, waiting for transfers between devices, body(): lax.all_to_all(real_part, 'seq', split_axis=1, concat_axis=2, tiled=True)  23.8 us
    all_to_all x1, waiting for transfers between devices, body(): lax.all_to_all(imag_part, 'seq', split_axis=1, concat_axis=2, tiled=True)  23.6 us
    all_to_all x1, starting transfers between devices, body(): lax.all_to_all(stacked.reshape(row_count, seq_count, block_len), 'seq', s...  23 us
    all_to_all x1, waiting for transfers between devices, body(): lax.all_to_all(back_real, 'seq', split_axis=2, concat_axis=1, tiled=True)  19.6 us
    all_to_all x1, waiting for transfers between devices, body(): lax.all_to_all(stacked.reshape(row_count, seq_count, block_len), 'seq', s...  19.3 us
    all_to_all x1, waiting for transfers between devices, body(): lax.all_to_all(back_imag, 'seq', split_axis=2, concat_axis=1, tiled=True)  19 us
    dot_general x20, matrix products, contract(): jnp.einsum(pattern, operand, weights, precision=lax.Precision.HIGHEST, pr...  11.7 us
  transfers between devices with their start and end apart: 5, of which 5 were waited for; matrix products, arithmetic and copies ran while one was open for 2% of the time, Pallas kernels for 0%

profile of v1, /device:TPU:1, one launch (start us, length us, event | category | flops | bytes accessed | tf_op | source)
XLA Modules:
  0.0 222.5 jit_solution(988739216877438854)
XLA Ops:
  0.6 0.0 copy-start.1
  0.6 0.0 copy-start
  0.6 0.9 copy.65
  1.5 0.0 copy-done.1
  1.6 0.1 copy.66
  1.7 0.0 copy-done
  1.7 0.1 copy.67
  1.8 0.8 reshape.209
  2.7 23.0 %all-to-all-start = ((f32[384,128,1]{0,2,1:T(1,128)}), f32[384,128,1]{0,2,1:T(1,128)S(1)}, u32[]{:S(2)}, u32[]{:S(2)}) async-start(f32[384,128,1]{0,2,1:T(1,128)} %reshape.209), calls=%async_computation | async-start | bytes 393216 | tf_op jit(solution)/shard_map/all_to_all | solution.py:89
  25.7 0.1 copy.64
  25.8 0.1 mul.547
  25.9 0.1 fusion.201
  26.0 19.3 %all-to-all-done = f32[384,128,1]{0,2,1:T(1,128)S(1)} async-done(((f32[384,128,1]{0,2,1:T(1,128)}), f32[384,128,1]{0,2,1:T(1,128)S(1)}, u32[]{:S(2)}, u32[]{:S(2)}) %all-to-all-start) | async-done | bytes 196640 | tf_op jit(solution)/shard_map/all_to_all | solution.py:89
  45.3 1.0 fusion
  46.3 1.0 add_bitcast_fusion.1
  47.3 1.2 copy.68
  48.5 7.5 %all-to-all-start.1 = ((f32[384,256,1]{0,2,1:T(1,128)}), f32[384,256,1]{0,2,1:T(1,128)S(1)}, u32[]{:S(2)}, u32[]{:S(2)}) async-start(f32[384,256,1]{0,2,1:T(1,128)} %copy.68), calls=%async_computation.1 | async-start | bytes 786432 | tf_op jit(solution)/shard_map/all_to_all | solution.py:106
  55.9 1.1 copy.71
  57.1 23.8 %all-to-all-done.1 = f32[384,256,1]{0,2,1:T(1,128)S(1)} async-done(((f32[384,256,1]{0,2,1:T(1,128)}), f32[384,256,1]{0,2,1:T(1,128)S(1)}, u32[]{:S(2)}, u32[]{:S(2)}) %all-to-all-start.1) | async-done | bytes 393248 | tf_op jit(solution)/shard_map/all_to_all | solution.py:106
  80.9 10.2 %all-to-all-start.2 = ((f32[384,256,1]{0,2,1:T(1,128)}), f32[384,256,1]{0,2,1:T(1,128)S(1)}, u32[]{:S(2)}, u32[]{:S(2)}) async-start(f32[384,256,1]{0,2,1:T(1,128)} %copy.71), calls=%async_computation.2 | async-start | bytes 786432 | tf_op jit(solution)/shard_map/all_to_all | solution.py:107
  91.1 0.1 broadcast_multiply_fusion
  91.2 0.1 copy.80
  91.3 0.1 fusion.105
  91.3 0.1 copy.81
  91.4 0.1 dynamic_slice.3
  91.5 0.1 fusion.114
  91.6 0.5 convolution_multiply_fusion.2
  92.2 23.6 %all-to-all-done.2 = f32[384,256,1]{0,2,1:T(1,128)S(1)} async-done(((f32[384,256,1]{0,2,1:T(1,128)}), f32[384,256,1]{0,2,1:T(1,128)S(1)}, u32[]{:S(2)}, u32[]{:S(2)}) %all-to-all-start.2) | async-done | bytes 393248 | tf_op jit(solution)/shard_map/all_to_all | solution.py:107
  115.8 0.5 convolution_multiply_fusion.3
  116.4 0.5 convolution_add_fusion.1
  116.9 0.6 add_bitcast_fusion
  117.5 0.6 convolution_multiply_fusion.1
  118.1 0.6 convolution_multiply_fusion
  118.7 0.6 convolution_subtract_fusion
  119.3 0.6 convolution_add_fusion
  119.8 0.1 multiply_subtract_fusion.2
  119.9 0.4 fusion.20
  120.3 0.4 fusion.21
  120.7 0.4 convolution_subtract_fusion.3
  121.1 0.5 multiply_subtract_fusion
  121.6 0.4 fusion.18
  122.0 0.4 fusion.14
  122.5 0.4 fusion.2
  122.9 0.4 fusion.1
  123.3 0.3 fusion.13
  123.6 0.9 copy.88
  124.5 10.1 %all-to-all-start.3 = ((f32[256,2,128]{0,1,2:T(2,128)}), f32[256,2,128]{0,1,2:T(2,128)S(1)}, u32[]{:S(2)}, u32[]{:S(2)}) async-start(f32[256,2,128]{0,1,2:T(2,128)} %copy.88), calls=%async_computation.3 | async-start | bytes 524288 | tf_op jit(solution)/shard_map/all_to_all | solution.py:132
  134.6 0.9 copy.89
  135.5 19.6 %all-to-all-done.3 = f32[256,2,128]{0,1,2:T(2,128)S(1)} async-done(((f32[256,2,128]{0,1,2:T(2,128)}), f32[256,2,128]{0,1,2:T(2,128)S(1)}, u32[]{:S(2)}, u32[]{:S(2)}) %all-to-all-start.3) | async-done | bytes 262176 | tf_op jit(solution)/shard_map/all_to_all | solution.py:132
  155.1 9.2 %all-to-all-start.4 = ((f32[256,2,128]{0,1,2:T(2,128)}), f32[256,2,128]{0,1,2:T(2,128)S(1)}, u32[]{:S(2)}, u32[]{:S(2)}) async-start(f32[256,2,128]{0,1,2:T(2,128)} %copy.89), calls=%async_computation.4 | async-start | bytes 524288 | tf_op jit(solution)/shard_map/all_to_all | solution.py:133
  164.4 0.2 reshape.215
  164.5 0.9 fusion.38
  165.5 19.0 %all-to-all-done.4 = f32[256,2,128]{0,1,2:T(2,128)S(1)} async-done(((f32[256,2,128]{0,1,2:T(2,128)}), f32[256,2,128]{0,1,2:T(2,128)S(1)}, u32[]{:S(2)}, u32[]{:S(2)}) %all-to-all-start.4) | async-done | bytes 262176 | tf_op jit(solution)/shard_map/all_to_all | solution.py:133
  184.5 0.2 reshape.216
  184.7 0.9 fusion.3
  185.7 0.1 copy.90
  185.8 25.7 %all_to_all.74 = f32[256,128,1]{0,2,1:T(1,128)S(1)} all-to-all(f32[256,128,1]{0,2,1:T(1,128)S(1)} %copy.90), channel_id=1, replica_groups=mesh['seq'=128,'batch'=4] {'seq'}, dimensions={1} | all-to-all | bytes 262144 | tf_op jit(solution)/shard_map/all_to_all | solution.py:138
  211.6 9.3 %all-gather = f32[512,128,1]{0,2,1:T(1,128)S(1)} all-gather(f32[128,128,1]{0,2,1:T(1,128)S(1)} %slice.43), channel_id=2, replica_groups=mesh['seq'=128,'batch'=4] {'batch'}, dimensions={0}, use_global_device_ids=true | all-gather | bytes 327680 | tf_op jit(solution)/shard_map/all_gather | solution.py:141
  220.8 0.2 reduce_sum.9
  221.0 0.7 copy.92
  221.8 0.7 copy.98
  (10 shorter events, 0.2 us)
Async XLA Ops:
  0.6 0.9 copy-start.1
  0.6 1.0 copy-start
  2.7 42.6 %all-to-all-start = ((f32[384,128,1]{0,2,1:T(1,128)}), f32[384,128,1]{0,2,1:T(1,128)S(1)}, u32[]{:S(2)}, u32[]{:S(2)}) async-start(f32[384,128,1]{0,2,1:T(1,128)} %reshape.209), calls=%async_computation | async-start | bytes 393216 | tf_op jit(solution)/shard_map/all_to_all | solution.py:89
  48.5 32.4 %all-to-all-start.1 = ((f32[384,256,1]{0,2,1:T(1,128)}), f32[384,256,1]{0,2,1:T(1,128)S(1)}, u32[]{:S(2)}, u32[]{:S(2)}) async-start(f32[384,256,1]{0,2,1:T(1,128)} %copy.68), calls=%async_computation.1 | async-start | bytes 786432 | tf_op jit(solution)/shard_map/all_to_all | solution.py:106
  80.9 34.9 %all-to-all-start.2 = ((f32[384,256,1]{0,2,1:T(1,128)}), f32[384,256,1]{0,2,1:T(1,128)S(1)}, u32[]{:S(2)}, u32[]{:S(2)}) async-start(f32[384,256,1]{0,2,1:T(1,128)} %copy.71), calls=%async_computation.2 | async-start | bytes 786432 | tf_op jit(solution)/shard_map/all_to_all | solution.py:107
  124.5 30.6 %all-to-all-start.3 = ((f32[256,2,128]{0,1,2:T(2,128)}), f32[256,2,128]{0,1,2:T(2,128)S(1)}, u32[]{:S(2)}, u32[]{:S(2)}) async-start(f32[256,2,128]{0,1,2:T(2,128)} %copy.88), calls=%async_computation.3 | async-start | bytes 524288 | tf_op jit(solution)/shard_map/all_to_all | solution.py:132
  155.1 29.4 %all-to-all-start.4 = ((f32[256,2,128]{0,1,2:T(2,128)}), f32[256,2,128]{0,1,2:T(2,128)S(1)}, u32[]{:S(2)}, u32[]{:S(2)}) async-start(f32[256,2,128]{0,1,2:T(2,128)} %copy.89), calls=%async_computation.4 | async-start | bytes 524288 | tf_op jit(solution)/shard_map/all_to_all | solution.py:133
